TPU v7x, 32 devices: a whole 2x2x4 slice. The times are simulated.
32 devices in a mesh: groups: 2 (over y), enc: 4 (over z), mp: 4 (over x, core).
Axes of the slice: x: 2, y: 2, z: 4, core: 2. Of those that a mesh axis runs over, the one named last changes fastest.
Arguments:
- hidden: bfloat16 [131072, 1024], P(('groups', 'enc'), 'mp'), parts along dimension 0, may hold values from -6 to 6
- proj_w: bfloat16 [1024, 128], P('mp'), may hold values from -0.1875 to 0.1875
- queries: bfloat16 [256, 32, 128], P(('groups', 'enc', 'mp')), parts along dimension 0, may hold values from -208 to 208
- lengths: int32 [512], P('groups'), parts along dimension 0, may hold values from 193 to 256, as said below
- candidates: int32 [256, 16], P(('groups', 'enc', 'mp')), parts along dimension 0, may hold values from 0 to 1023, as said below
Outputs:
- losses: float32 [256], P(('groups', 'enc', 'mp')), parts along dimension 0
- grad_w: float32 [2048, 128], P(('groups', 'mp')), parts along dimension 0
There are 2 independent parts, one for each index of `groups`. A program takes and returns all parts, laid end to end along the dimension named above; an argument that names none is the same for every part. Nothing has to cross between parts.
Inputs may be any that keep to these rules, and one draw needn't show every extreme that they name: Entries are global block numbers of this part. Of the candidates of the 8 queries of one device (aligned rows), at most 16 lie in the 64 blocks of any one device along enc+mp, where device k holds blocks k * 64 to (k + 1) * 64 - 1; some device receives exactly 16 from every device. Blocks may repeat. `lengths`: some passage has 256 tokens and some has 193.
All inputs are finite; a program needn't handle non-finite values.
Results may differ from a plain program's by a relative error of at most 0.0013.
The roundings to bfloat16 on the way count: a program that leaves them out, or rounds other values in their place, can miss the bound.
Values may be sent and summed in bfloat16 or wider, within the bound.
No kernel may reach another device: no remote copies, remote signals or barrier semaphores. Data moves between devices by JAX's collectives and lax.ppermute only.
A program may use at most 128 MiB of HBM per device.

v0:
```python
import jax
import jax.numpy as jnp
from jax import lax
from jax.sharding import PartitionSpec as P

L = 256
BLK = 64


def block_valid(block_ids, lengths):
    per_passage = L // BLK
    passage = block_ids // per_passage
    within = block_ids % per_passage
    positions = within[..., None] * BLK + jnp.arange(BLK, dtype=jnp.int32)
    return positions < lengths[passage][..., None]


def soft_max_sim(sim_tile, valid_mask):
    masked = jnp.where(valid_mask, sim_tile, jnp.float32(-1e30))
    peak = jnp.max(masked, -1, keepdims=True)
    shifted = jnp.exp(masked - peak)
    running = jnp.sum(shifted, -1, keepdims=True)
    scores = jnp.mean(peak[..., 0] + jnp.log(running[..., 0]), -1)
    weights = (shifted / running).astype(jnp.bfloat16)
    return (scores, weights)


def loss_terms(scores):
    margins = scores[:, 1:] - scores[:, :1]
    losses = jnp.mean(jax.nn.softplus(margins), 1)
    slopes = jax.nn.sigmoid(margins) / (scores.shape[1] - 1)
    d_score = jnp.concatenate([-jnp.sum(slopes, 1, keepdims=True), slopes], 1)
    return (losses, d_score)


def left_product(left, right):
    return lax.dot_general(
        left, right, (((0,), (0,)), ((), ())), preferred_element_type=jnp.float32
    )


def local(hidden, proj_w, queries, lengths, candidates):
    mp_count = lax.axis_size("mp")
    owners = lax.axis_size("enc") * mp_count
    row_share = hidden.shape[0] // mp_count
    emb_width = proj_w.shape[1]
    qry_dev = queries.shape[0]
    query_len = queries.shape[1]
    cand_count = candidates.shape[1]
    blk_dev = row_share // BLK
    slot_count = qry_dev * cand_count
    capacity = 2 * slot_count // owners
    me = lax.axis_index("enc") * mp_count + lax.axis_index("mp")
    all_queries = lax.all_gather(queries, ("enc", "mp"), axis=0, tiled=True)
    all_cand = lax.all_gather(candidates, ("enc", "mp"), axis=0, tiled=True)
    all_cand = all_cand.reshape(owners, slot_count)
    e_pre = lax.psum_scatter(
        jnp.dot(hidden, proj_w, preferred_element_type=jnp.float32),
        "mp",
        scatter_dimension=0,
        tiled=True,
    )
    scale = lax.rsqrt(jnp.sum(e_pre * e_pre, -1, keepdims=True) + 1e-06)
    embedded = (e_pre * scale).astype(jnp.bfloat16)
    local_blocks = embedded.reshape(blk_dev, BLK, emb_width)
    slot_ids = jnp.arange(slot_count, dtype=jnp.int32)
    mine = all_cand // blk_dev == me
    rank = jnp.cumsum(mine.astype(jnp.int32), axis=1) - 1
    ranks = jnp.arange(capacity, dtype=jnp.int32)
    pick = mine[:, None, :] & (rank[:, None, :] == ranks[None, :, None])
    valid = jnp.any(pick, axis=2)
    slot_of = jnp.sum(jnp.where(pick, slot_ids[None, None, :], 0), axis=2).astype(jnp.int32)
    block_of = jnp.take_along_axis(all_cand, slot_of, axis=1)
    local_of = block_of % blk_dev
    query_of = jnp.arange(owners, dtype=jnp.int32)[:, None] * qry_dev + slot_of // cand_count
    tiles = local_blocks[local_of]
    q_e = all_queries[query_of]
    valid_mask = block_valid(block_of, lengths)
    sim_tile = jnp.einsum("scie,scje->scij", q_e, tiles, preferred_element_type=jnp.float32)
    scores, weights = soft_max_sim(sim_tile, valid_mask[:, :, None, :])
    placed = jnp.sum(jnp.where(pick, scores[:, :, None], jnp.float32(0)), axis=1)
    all_scores = lax.psum(placed, ("enc", "mp")).reshape(owners * qry_dev, cand_count)
    all_losses, d_score = loss_terms(all_scores)
    losses = lax.dynamic_slice_in_dim(all_losses, me * qry_dev, qry_dev)
    d_e = jnp.take_along_axis(d_score.reshape(owners, slot_count), slot_of, axis=1)
    d_e = jnp.where(valid, d_e, jnp.float32(0))
    occ_grad = jnp.einsum("scij,scie->scje", weights, q_e, preferred_element_type=jnp.float32)
    occ_grad = (occ_grad * (d_e / query_len)[:, :, None, None]).astype(jnp.bfloat16)
    onehot = (local_of[:, :, None] == jnp.arange(blk_dev, dtype=jnp.int32)) & valid[:, :, None]
    grad_emb = jnp.einsum(
        "scb,scx->bx",
        onehot.astype(jnp.bfloat16),
        occ_grad.reshape(owners, capacity, BLK * emb_width),
        preferred_element_type=jnp.float32,
    )
    grad_flat = grad_emb.reshape(row_share, emb_width)
    dot_e = jnp.sum(e_pre * grad_flat, -1, keepdims=True)
    de_pre = (scale * grad_flat - e_pre * (scale * scale * scale) * dot_e).astype(jnp.bfloat16)
    partial_w = left_product(hidden, lax.all_gather(de_pre, "mp", axis=0, tiled=True))
    grad_w = lax.psum(partial_w, "enc")
    return (losses, grad_w)


def solution(mesh):
    return jax.shard_map(
        local,
        mesh=mesh,
        in_specs=(
            P(("groups", "enc"), "mp"),
            P("mp", None),
            P(("groups", "enc", "mp"), None, None),
            P("groups"),
            P(("groups", "enc", "mp"), None),
        ),
        out_specs=(P(("groups", "enc", "mp")), P(("groups", "mp"), None)),
        check_vma=False,
    )
```

profile of v0, /device:TPU:0, one launch (start us, length us, event | category | flops | bytes accessed | tf_op | source)
XLA Modules:
  0.0 255.7 jit_solution(6291594766435006573)
XLA Ops:
  8.1 0.7 all-gather.3.cloned.1.call-update
  8.8 8.9 %fusion.27 = f32[16384,128]{1,0:T(8,128)} fusion(bf16[16384,256]{1,0:T(8,128)(2,1)} %param.5, bf16[256,128]{1,0:T(8,128)(2,1)S(1)} %copy-done), kind=kOutput, calls=%fused_computation.94 | convolution fusion | flops 1073741824 | bytes 16842752 | tf_op jit(solution)/shard_map/dot_general | solution.py:58
  17.9 0.6 copy-done.5
  18.5 23.4 %all_gather.9 = s32[128,16]{1,0:T(8,128)S(1)} all-gather(s32[8,16]{1,0:T(8,128)S(1)} %copy-done.5), channel_id=1, replica_groups=mesh['groups'=2,'enc'=4,'mp'=4] {'enc','mp'}, dimensions={0}, use_global_device_ids=true | all-gather | bytes 8704 | tf_op jit(solution)/shard_map/all_gather | solution.py:55
  41.8 0.1 reshape.380
  41.9 0.3 reduce_window_sum.11
  42.2 0.4 select_reduce_fusion.2
  42.6 0.1 reshape.410
  42.7 1.9 gather_fusion.3
  44.6 0.1 reshape.413
  44.6 0.1 gather.20
  44.7 0.4 fusion.7
  45.1 0.1 copy.34
  45.3 0.1 compare_select_fusion.3
  45.4 0.1 reshape.388
  45.4 0.1 reshape.404
  45.5 0.1 reshape.396
  45.6 1.9 gather_fusion
  47.6 0.1 reshape.387
  47.7 0.1 add_compare_fusion
  47.8 3.8 %all-gather.3.cloned.1.call-done = bf16[128,32,128]{2,1,0:T(8,128)(2,1)} async-done(((bf16[8,32,128]{2,1,0:T(8,128)(2,1)}), bf16[128,32,128]{2,1,0:T(8,128)(2,1)}) %all-gather.3.cloned.1.call-update) | async-done | bytes 1048592 | tf_op jit(solution)/shard_map/all_gather | solution.py:54
  51.6 2.2 gather_fusion.1
  53.9 38.4 %reduce-scatter.2.cloned.1.call-done = f32[4096,128]{1,0:T(8,128)} async-done(((f32[16384,128]{1,0:T(8,128)}), f32[4096,128]{1,0:T(8,128)}) %reduce-scatter.2.cloned.1.call-update) | async-done | bytes 2097168 | tf_op jit(solution)/shard_map/reduce_scatter | solution.py:57
  92.3 2.2 multiply_reduce_fusion.1
  94.5 1.9 multiply_convert_fusion.1
  96.4 3.0 %gather_fusion.2 = bf16[256,64,128]{2,1,0:T(8,128)(2,1)} fusion(bf16[64,64,128]{2,1,0:T(8,128)(2,1)S(1)} %bitcast.55, s32[1024]{0:T(1024)S(1)} %pad_clamp_fusion), kind=kCustom, calls=%fused_computation.2 | custom fusion | bytes 8389632 | tf_op jit(solution)/shard_map/gather | solution.py:76
  99.5 4.6 %select_reduce_fusion = (f32[16,16,32]{2,1,0:T(8,128)S(1)}, f32[16,16,32,64]{3,2,1,0:T(8,128)S(1)}) fusion(pred[16,16,64]{2,1,0:T(8,128)(4,1)S(1)} %add_compare_fusion, bf16[16,16,32,128]{3,2,1,0:T(8,128)(2,1)S(1)} %bitcast.57, bf16[16,16,64,128]{3,2,1,0:T(8,128)(2,1)} %bitcast.56), kind=kOutput, calls=%fused_computation.10 | convolution fusion | flops 135258112 | bytes 8437760 | tf_op jit(solution)/shard_map/scie,scje->scij/dot_general | solution.py:79
  104.1 2.0 copy-done.4
  106.0 2.4 fusion.1
  108.5 0.1 add_reduce_fusion
  108.6 0.1 select_reduce_fusion.1
  108.7 0.1 reshape.382
  108.9 32.9 %psum.14 = f32[128,16]{0,1:T(8,128)S(1)} all-reduce(f32[128,16]{0,1:T(8,128)S(1)} %copy.32), channel_id=1, replica_groups=mesh['groups'=2,'enc'=4,'mp'=4] {'enc','mp'}, use_global_device_ids=true, to_apply=%region_8.9 | all-reduce | flops 2048 | bytes 16384 | tf_op jit(solution)/shard_map/psum | solution.py:82
  141.8 0.1 copy.35
  141.9 0.1 reshape.383
  142.0 1.9 gather_fusion.4
  143.9 0.1 reshape.419
  144.0 8.0 %multiply_convert_fusion = bf16[16,16,64,128]{3,2,1,0:T(8,128)(2,1)} fusion(f32[16,16]{1,0:T(8,128)S(1)} %select_multiply_fusion, bf16[16,16,32,128]{3,2,1,0:T(8,128)(2,1)S(1)} %bitcast.58, f32[16,16,32,64]{3,2,1,0:T(8,128)} %copy-done.4, f32[16,16,32]{2,1,0:T(8,128)S(1)} %fusion.1, f32[16,16,32]{2,1,0:T(8,128)S(1)} %get-tuple-element.26, ...), kind=kOutput, calls=%fused_computation.6 | convolution fusion | flops 140509184 | bytes 8471552 | tf_op jit(solution)/shard_map/scij,scie->scje/dot_general | solution.py:87
  152.0 7.3 %reshape.384 = bf16[16,16,8192]{2,1,0:T(8,128)(2,1)} reshape(bf16[16,16,64,128]{3,2,1,0:T(8,128)(2,1)} %multiply_convert_fusion) | data formatting | bytes 8388608 | tf_op jit(solution)/shard_map/reshape | solution.py:93
  159.3 6.3 %convolution_bitcast_fusion = f32[64,8192]{1,0:T(8,128)} fusion(bf16[16,16,8192]{2,1,0:T(8,128)(2,1)} %reshape.384, s32[16,16]{0,1:T(8,128)S(1)} %copy.33, pred[16,16]{0,1:T(8,128)(4,1)S(1)} %copy.34), kind=kOutput, calls=%fused_computation.5 | convolution fusion | flops 268468224 | bytes 6292736 | tf_op jit(solution)/shard_map/scb,scx->bx/dot_general | solution.py:90
  165.6 2.7 %reshape.385 = f32[4096,128]{1,0:T(8,128)} reshape(f32[64,8192]{1,0:T(8,128)} %convolution_bitcast_fusion) | data formatting | bytes 4194304 | tf_op jit(solution)/shard_map/reshape | solution.py:96
  168.3 2.4 multiply_reduce_fusion
  170.6 2.9 %subtract_convert_fusion = bf16[4096,128]{1,0:T(8,128)(2,1)} fusion(f32[4096,128]{1,0:T(8,128)S(1)} %copy-done.2, f32[4096,128]{1,0:T(8,128)S(1)} %copy-done.3, f32[4096]{0:T(1024)S(1)} %multiply_reduce_fusion, f32[4096]{0:T(1024)S(1)} %get-tuple-element.20, f32[4096]{0:T(1024)S(1)} %get-tuple-element.21), kind=kLoop, calls=%fused_computation.12 | loop fusion | flops 2621440 | bytes 5292032 | tf_op jit(solution)/shard_map/convert_element_type | solution.py:98
  173.6 31.6 %all-gather.5.cloned.1.call-done = bf16[16384,128]{1,0:T(8,128)(2,1)} async-done(((bf16[4096,128]{1,0:T(8,128)(2,1)}), bf16[16384,128]{1,0:T(8,128)(2,1)}) %all-gather.5.cloned.1.call-update) | async-done | bytes 4194320 | tf_op jit(solution)/shard_map/all_gather | solution.py:99
  205.2 6.8 %convolution_bitcast_fusion.1 = f32[256,128]{0,1:T(8,128)} fusion(bf16[16384,128]{1,0:T(8,128)(2,1)} %all-gather.5.cloned.1.call-done, bf16[16384,256]{1,0:T(8,128)(2,1)} %param.5), kind=kOutput, calls=%fused_computation.20 | convolution fusion | flops 1073741824 | bytes 12713984 | tf_op jit(solution)/shard_map/dot_general | solution.py:37
  212.1 0.6 dynamic_slice.3
  212.7 34.0 %all-reduce.2.cloned.1.call-done = f32[256,128]{0,1:T(8,128)} async-done(((f32[256,128]{0,1:T(8,128)}), f32[256,128]{0,1:T(8,128)}) %all-reduce.2.cloned.1.call-update) | async-done | bytes 131088 | tf_op jit(solution)/shard_map/psum | solution.py:100
  246.7 1.7 copy.37
  (36 shorter events, 0.6 us)
Async XLA Ops:
  8.0 0.8 copy-start
  8.0 43.6 %all-gather.3.cloned.1.call-start = ((), (), s32[]{:S(2)}) async-start(), calls=%async_computation.1 | async-start | bytes 1114112 | tf_op jit(solution)/shard_map/all_gather | solution.py:54
  8.7 83.5 %reduce-scatter.2.cloned.1.call-start = ((), (), s32[]{:S(2)}) async-start(), calls=%async_computation.2 | async-start | bytes 10485760 | tf_op jit(solution)/shard_map/reduce_scatter | solution.py:57
  17.8 0.7 copy-start.5
  17.8 187.4 %all-gather.5.cloned.1.call-start = ((), (), s32[]{:S(2)}) async-start(), calls=%async_computation.3 | async-start | bytes 5242880 | tf_op jit(solution)/shard_map/all_gather | solution.py:99
  42.7 2.9 %copy-start.1 = (s32[256]{0:T(256)S(1)}, s32[256]{0:T(256)}, u32[]{:S(2)}) copy-start(s32[256]{0:T(256)} %param.8) | copy-start | bytes 3076
  104.1 2.0 copy-start.4
  159.3 9.0 %copy-start.2 = (f32[4096,128]{1,0:T(8,128)S(1)}, f32[4096,128]{1,0:T(8,128)}, u32[]{:S(2)}) copy-start(f32[4096,128]{1,0:T(8,128)} %reduce-scatter.2.cloned.1.call-done) | copy-start | bytes 6291460
  168.3 2.4 copy-start.3
  173.5 73.1 %all-reduce.2.cloned.1.call-start = ((), (), s32[]{:S(2)}) async-start(), calls=%async_computation.4 | async-start | bytes 262144 | tf_op jit(solution)/shard_map/psum | solution.py:100
Sparse Core Ops, SparseCore 0:
  11.0 40.5 all-gather.2
  212.2 34.4 all-reduce.1
Sparse Core Ops, SparseCore 1:
  17.9 74.3 reduce-scatter.1
  173.6 31.5 all-gather.4
where the time goes:
time: 256 us
  waiting for transfers between devices  109 us (43%)
  blocking collectives  56.2 us (22%)
  matrix products  34.7 us (14%)
  local copies, waits for them, and re-layouts  27 us (11%)
  between operations  15.7 us (6%)
  other arithmetic  13.4 us (5%)
    reduce_scatter x1, waiting for transfers between devices, local(): lax.psum_scatter(jnp.dot(hidden, proj_w, preferred_element_type=jnp.float...  38.4 us
    psum x1, waiting for transfers between devices, local(): grad_w = lax.psum(partial_w, 'enc')  34 us
    psum x1, blocking collectives, local(): lax.psum(placed, ('enc', 'mp')).reshape(owners * qry_dev, cand_count)  32.9 us
    all_gather x1, waiting for transfers between devices, local(): lax.all_gather(de_pre, 'mp', axis=0, tiled=True)  31.6 us
    all_gather x1, blocking collectives, local(): all_cand = lax.all_gather(candidates, ('enc', 'mp'), axis=0, tiled=True)  23.4 us
    dot_general x1, matrix products, local(): jnp.dot(hidden, proj_w, preferred_element_type=jnp.float32)  8.94 us
    dot_general x1, matrix products, local(): jnp.einsum('scij,scie->scje', weights, q_e, preferred_element_type=jnp.fl...  8 us
    reshape x1, local copies, waits for them, and re-layouts, local(): occ_grad.reshape(owners, capacity, BLK * emb_width)  7.31 us
  transfers between devices with their start and end apart: 4, of which 4 were waited for; matrix products, arithmetic and copies ran while one was open for 7% of the time, Pallas kernels for 0%

commit v1 on v0

--- a/solution.py
+++ b/solution.py
@@ -79,7 +79,7 @@
     sim_tile = jnp.einsum("scie,scje->scij", q_e, tiles, preferred_element_type=jnp.float32)
     scores, weights = soft_max_sim(sim_tile, valid_mask[:, :, None, :])
     placed = jnp.sum(jnp.where(pick, scores[:, :, None], jnp.float32(0)), axis=1)
-    all_scores = lax.psum(placed, ("enc", "mp")).reshape(owners * qry_dev, cand_count)
+    all_scores = lax.psum(lax.psum(placed, "mp"), "enc").reshape(owners * qry_dev, cand_count)
     all_losses, d_score = loss_terms(all_scores)
     losses = lax.dynamic_slice_in_dim(all_losses, me * qry_dev, qry_dev)
     d_e = jnp.take_along_axis(d_score.reshape(owners, slot_count), slot_of, axis=1)

time: 256 us -> 242 us (0.945)
  blocking collectives: 56.2 us -> 41.5 us
    psum x1 -> x2, blocking collectives: 32.9 us -> 18.1 us  [the longest x1 12.3 us: local(): lax.psum(lax.psum(placed, 'mp'), 'enc')]
where the time goes in v1:
time: 242 us; the launch traced here: 241 us
  waiting for transfers between devices  109 us (45%)
  blocking collectives  41.5 us (17%)
  matrix products  34.7 us (14%)
  local copies, waits for them, and re-layouts  27 us (11%)
  between operations  15.7 us (6%)
  other arithmetic  13.4 us (6%)
    reduce_scatter x1, waiting for transfers between devices, local(): lax.psum_scatter(jnp.dot(hidden, proj_w, preferred_element_type=jnp.float...  38.4 us
    psum x1, waiting for transfers between devices, local(): grad_w = lax.psum(partial_w, 'enc')  34 us
    all_gather x1, waiting for transfers between devices, local(): lax.all_gather(de_pre, 'mp', axis=0, tiled=True)  32.1 us
    all_gather x1, blocking collectives, local(): all_cand = lax.all_gather(candidates, ('enc', 'mp'), axis=0, tiled=True)  23.4 us
    psum x1, blocking collectives, local(): lax.psum(lax.psum(placed, 'mp'), 'enc')  12.3 us
    dot_general x1, matrix products, local(): jnp.dot(hidden, proj_w, preferred_element_type=jnp.float32)  8.94 us
    dot_general x1, matrix products, local(): jnp.einsum('scij,scie->scje', weights, q_e, preferred_element_type=jnp.fl...  8 us
    reshape x1, local copies, waits for them, and re-layouts, local(): occ_grad.reshape(owners, capacity, BLK * emb_width)  7.31 us
  transfers between devices with their start and end apart: 4, of which 4 were waited for; matrix products, arithmetic and copies ran while one was open for 7% of the time, Pallas kernels for 0%

profile of v1, /device:TPU:0, one launch (start us, length us, event | category | flops | bytes accessed | tf_op | source)
XLA Modules:
  0.0 241.5 jit_solution(1293869924825637662)
XLA Ops:
  8.1 0.7 all-gather.3.cloned.1.call-update
  8.8 8.9 %fusion.27 = f32[16384,128]{1,0:T(8,128)} fusion(bf16[16384,256]{1,0:T(8,128)(2,1)} %param.5, bf16[256,128]{1,0:T(8,128)(2,1)S(1)} %copy-done), kind=kOutput, calls=%fused_computation.94 | convolution fusion | flops 1073741824 | bytes 16842752 | tf_op jit(solution)/shard_map/dot_general | solution.py:58
  17.9 0.6 copy-done.5
  18.5 23.4 %all_gather.9 = s32[128,16]{1,0:T(8,128)S(1)} all-gather(s32[8,16]{1,0:T(8,128)S(1)} %copy-done.5), channel_id=1, replica_groups=mesh['groups'=2,'enc'=4,'mp'=4] {'enc','mp'}, dimensions={0}, use_global_device_ids=true | all-gather | bytes 8704 | tf_op jit(solution)/shard_map/all_gather | solution.py:55
  41.8 0.1 reshape.380
  41.9 0.3 reduce_window_sum.11
  42.2 0.4 select_reduce_fusion.2
  42.6 0.1 reshape.410
  42.7 1.9 gather_fusion.3
  44.6 0.1 reshape.413
  44.6 0.1 gather.20
  44.7 0.4 fusion.7
  45.1 0.1 copy.34
  45.3 0.1 compare_select_fusion.3
  45.4 0.1 reshape.388
  45.4 0.1 reshape.404
  45.5 0.1 reshape.396
  45.6 1.9 gather_fusion
  47.6 0.1 reshape.387
  47.7 0.1 add_compare_fusion
  47.8 3.8 %all-gather.3.cloned.1.call-done = bf16[128,32,128]{2,1,0:T(8,128)(2,1)} async-done(((bf16[8,32,128]{2,1,0:T(8,128)(2,1)}), bf16[128,32,128]{2,1,0:T(8,128)(2,1)}) %all-gather.3.cloned.1.call-update) | async-done | bytes 1048592 | tf_op jit(solution)/shard_map/all_gather | solution.py:54
  51.6 2.2 gather_fusion.1
  53.9 38.4 %reduce-scatter.2.cloned.1.call-done = f32[4096,128]{1,0:T(8,128)} async-done(((f32[16384,128]{1,0:T(8,128)}), f32[4096,128]{1,0:T(8,128)}) %reduce-scatter.2.cloned.1.call-update) | async-done | bytes 2097168 | tf_op jit(solution)/shard_map/reduce_scatter | solution.py:57
  92.3 2.2 multiply_reduce_fusion.1
  94.5 1.9 multiply_convert_fusion.1
  96.4 3.0 %gather_fusion.2 = bf16[256,64,128]{2,1,0:T(8,128)(2,1)} fusion(bf16[64,64,128]{2,1,0:T(8,128)(2,1)S(1)} %bitcast.55, s32[1024]{0:T(1024)S(1)} %pad_clamp_fusion), kind=kCustom, calls=%fused_computation.2 | custom fusion | bytes 8389632 | tf_op jit(solution)/shard_map/gather | solution.py:76
  99.5 4.6 %select_reduce_fusion = (f32[16,16,32]{2,1,0:T(8,128)S(1)}, f32[16,16,32,64]{3,2,1,0:T(8,128)S(1)}) fusion(pred[16,16,64]{2,1,0:T(8,128)(4,1)S(1)} %add_compare_fusion, bf16[16,16,32,128]{3,2,1,0:T(8,128)(2,1)S(1)} %bitcast.57, bf16[16,16,64,128]{3,2,1,0:T(8,128)(2,1)} %bitcast.56), kind=kOutput, calls=%fused_computation.10 | convolution fusion | flops 135258112 | bytes 8437760 | tf_op jit(solution)/shard_map/scie,scje->scij/dot_general | solution.py:79
  104.1 2.0 copy-done.4
  106.0 2.4 fusion.1
  108.5 0.1 add_reduce_fusion
  108.6 0.1 select_reduce_fusion.1
  108.7 5.9 %psum.21 = f32[16,128]{1,0:T(8,128)S(1)} all-reduce(f32[16,128]{1,0:T(8,128)S(1)} %select_reduce_fusion.1), channel_id=1, replica_groups=mesh['groups'=2,'enc'=4,'mp'=4] {'mp'}, use_global_device_ids=true, to_apply=%region_8.9 | all-reduce | flops 2048 | bytes 16384 | tf_op jit(solution)/shard_map/psum | solution.py:82
  114.7 12.3 %psum.22 = f32[128,16]{0,1:T(8,128)S(1)} all-reduce(f32[128,16]{0,1:T(8,128)S(1)} %copy.32), channel_id=1, replica_groups=mesh['groups'=2,'enc'=4,'mp'=4] {'enc'}, use_global_device_ids=true, to_apply=%region_9.10 | all-reduce | flops 2048 | bytes 16384 | tf_op jit(solution)/shard_map/psum | solution.py:82
  127.1 0.1 copy.35
  127.2 0.1 reshape.383
  127.3 1.9 gather_fusion.4
  129.2 0.1 reshape.419
  129.3 8.0 %multiply_convert_fusion = bf16[16,16,64,128]{3,2,1,0:T(8,128)(2,1)} fusion(f32[16,16]{1,0:T(8,128)S(1)} %select_multiply_fusion, bf16[16,16,32,128]{3,2,1,0:T(8,128)(2,1)S(1)} %bitcast.58, f32[16,16,32,64]{3,2,1,0:T(8,128)} %copy-done.4, f32[16,16,32]{2,1,0:T(8,128)S(1)} %fusion.1, f32[16,16,32]{2,1,0:T(8,128)S(1)} %get-tuple-element.26, ...), kind=kOutput, calls=%fused_computation.6 | convolution fusion | flops 140509184 | bytes 8471552 | tf_op jit(solution)/shard_map/scij,scie->scje/dot_general | solution.py:87
  137.3 7.3 %reshape.384 = bf16[16,16,8192]{2,1,0:T(8,128)(2,1)} reshape(bf16[16,16,64,128]{3,2,1,0:T(8,128)(2,1)} %multiply_convert_fusion) | data formatting | bytes 8388608 | tf_op jit(solution)/shard_map/reshape | solution.py:93
  144.6 6.3 %convolution_bitcast_fusion = f32[64,8192]{1,0:T(8,128)} fusion(bf16[16,16,8192]{2,1,0:T(8,128)(2,1)} %reshape.384, s32[16,16]{0,1:T(8,128)S(1)} %copy.33, pred[16,16]{0,1:T(8,128)(4,1)S(1)} %copy.34), kind=kOutput, calls=%fused_computation.5 | convolution fusion | flops 268468224 | bytes 6292736 | tf_op jit(solution)/shard_map/scb,scx->bx/dot_general | solution.py:90
  150.9 2.7 %reshape.385 = f32[4096,128]{1,0:T(8,128)} reshape(f32[64,8192]{1,0:T(8,128)} %convolution_bitcast_fusion) | data formatting | bytes 4194304 | tf_op jit(solution)/shard_map/reshape | solution.py:96
  153.6 2.4 multiply_reduce_fusion
  155.9 2.9 %subtract_convert_fusion = bf16[4096,128]{1,0:T(8,128)(2,1)} fusion(f32[4096,128]{1,0:T(8,128)S(1)} %copy-done.2, f32[4096,128]{1,0:T(8,128)S(1)} %copy-done.3, f32[4096]{0:T(1024)S(1)} %multiply_reduce_fusion, f32[4096]{0:T(1024)S(1)} %get-tuple-element.20, f32[4096]{0:T(1024)S(1)} %get-tuple-element.21), kind=kLoop, calls=%fused_computation.12 | loop fusion | flops 2621440 | bytes 5292032 | tf_op jit(solution)/shard_map/convert_element_type | solution.py:98
  158.9 32.1 %all-gather.5.cloned.1.call-done = bf16[16384,128]{1,0:T(8,128)(2,1)} async-done(((bf16[4096,128]{1,0:T(8,128)(2,1)}), bf16[16384,128]{1,0:T(8,128)(2,1)}) %all-gather.5.cloned.1.call-update) | async-done | bytes 4194320 | tf_op jit(solution)/shard_map/all_gather | solution.py:99
  190.9 6.8 %convolution_bitcast_fusion.1 = f32[256,128]{0,1:T(8,128)} fusion(bf16[16384,128]{1,0:T(8,128)(2,1)} %all-gather.5.cloned.1.call-done, bf16[16384,256]{1,0:T(8,128)(2,1)} %param.5), kind=kOutput, calls=%fused_computation.20 | convolution fusion | flops 1073741824 | bytes 12713984 | tf_op jit(solution)/shard_map/dot_general | solution.py:37
  197.8 0.6 dynamic_slice.3
  198.4 34.0 %all-reduce.2.cloned.1.call-done = f32[256,128]{0,1:T(8,128)} async-done(((f32[256,128]{0,1:T(8,128)}), f32[256,128]{0,1:T(8,128)}) %all-reduce.2.cloned.1.call-update) | async-done | bytes 131088 | tf_op jit(solution)/shard_map/psum | solution.py:100
  232.4 1.7 copy.37
  (37 shorter events, 0.6 us)
Async XLA Ops:
  8.0 0.8 copy-start
  8.0 43.6 %all-gather.3.cloned.1.call-start = ((), (), s32[]{:S(2)}) async-start(), calls=%async_computation.1 | async-start | bytes 1114112 | tf_op jit(solution)/shard_map/all_gather | solution.py:54
  8.7 83.5 %reduce-scatter.2.cloned.1.call-start = ((), (), s32[]{:S(2)}) async-start(), calls=%async_computation.2 | async-start | bytes 10485760 | tf_op jit(solution)/shard_map/reduce_scatter | solution.py:57
  17.8 0.7 copy-start.5
  17.8 173.1 %all-gather.5.cloned.1.call-start = ((), (), s32[]{:S(2)}) async-start(), calls=%async_computation.3 | async-start | bytes 5242880 | tf_op jit(solution)/shard_map/all_gather | solution.py:99
  42.7 2.9 %copy-start.1 = (s32[256]{0:T(256)S(1)}, s32[256]{0:T(256)}, u32[]{:S(2)}) copy-start(s32[256]{0:T(256)} %param.8) | copy-start | bytes 3076
  104.1 2.0 copy-start.4
  144.6 9.0 %copy-start.2 = (f32[4096,128]{1,0:T(8,128)S(1)}, f32[4096,128]{1,0:T(8,128)}, u32[]{:S(2)}) copy-start(f32[4096,128]{1,0:T(8,128)} %reduce-scatter.2.cloned.1.call-done) | copy-start | bytes 6291460
  153.5 2.4 copy-start.3
  158.8 73.6 %all-reduce.2.cloned.1.call-start = ((), (), s32[]{:S(2)}) async-start(), calls=%async_computation.4 | async-start | bytes 262144 | tf_op jit(solution)/shard_map/psum | solution.py:100
Sparse Core Ops, SparseCore 0:
  11.0 40.5 all-gather.2
  197.9 34.4 all-reduce.1
Sparse Core Ops, SparseCore 1:
  17.9 74.3 reduce-scatter.1
  158.9 32.0 all-gather.4
